TPU v7x, 512 devices: a whole 4x8x8 slice. The times are simulated.
512 devices in a mesh: depth: 16 (over x_hi, y), scan: 32 (over z, x_lo, core).
Axes of the slice: x: 4 (x_hi: 2, x_lo: 2; x = x_hi * 2 + x_lo), y: 8, z: 8, core: 2. Of those that a mesh axis runs over, the one named last changes fastest.
Arguments:
- object_slice: bfloat16 [2, 4, 512, 2048], P(None, None, 'depth', 'scan'), may hold values from -4 to 4
- probe_field: bfloat16 [2, 512, 512], replicated, may hold values from -2 to 2
- offsets: int32 [64, 2], replicated, may hold values from 0 to 1536
- assignment: int32 [64], P('scan'), may hold values from 0 to 63, each once
- intensities: float32 [64, 512, 512], P('scan', 'depth'), may hold values from 0 to 3
Outputs:
- object_grad: float32 [2, 4, 512, 2048], P(None, None, 'depth', 'scan')
- probe_grad: float32 [2, 512, 512], P(None, 'depth')
Inputs may be any that keep to these rules, and one draw needn't show every extreme that they name: `offsets`: each window lies inside the object window. `assignment`: every position stands in exactly one slot; slots s * 2 to s * 2 + 1 lie on index s of scan.
All inputs are finite; a program needn't handle non-finite values.
Results may differ from a plain program's by a relative error of at most 0.0003.
Values may be sent and summed in bfloat16 or wider, within the bound.
No kernel may reach another device: no remote copies, remote signals or barrier semaphores. Data moves between devices by JAX's collectives and lax.ppermute only.
A program may use at most 64 MiB of HBM per device.

v0:
```python
import math
import jax
import jax.numpy as jnp
from jax import lax
from jax.sharding import PartitionSpec as P

fresnel_scale = 4


def from_behind(block, axis, distance):
    devices = range(lax.axis_size(axis))
    route = [((i - distance) % len(devices), i) for i in devices]
    return lax.ppermute(block, axis, route)


def dft_table(size):
    index = jnp.arange(size, dtype=jnp.int32)
    turns = index[:, None] * index[None, :] % size
    angle = 2.0 * math.pi / size * turns.astype(jnp.float32)
    norm = 1.0 / math.sqrt(size)
    return (jnp.cos(angle) * norm, -jnp.sin(angle) * norm)


def chirp_phase(index, size):
    centred = index - size // 2
    period = 2 * fresnel_scale * size
    phase = centred * centred % period
    angle = math.pi / (fresnel_scale * size) * phase.astype(jnp.float32)
    return (jnp.cos(angle), jnp.sin(angle))


def contract(form, left_side, right_side):
    return jnp.einsum(
        form,
        left_side,
        right_side,
        precision=lax.Precision.HIGHEST,
        preferred_element_type=jnp.float32,
    )


def complex_mix(form, left_re, left_im, right_re, right_im):
    real_part = contract(form, left_re, right_re) - contract(form, left_im, right_im)
    imag_part = contract(form, left_re, right_im) + contract(form, left_im, right_re)
    return (real_part, imag_part)


def on_device(object_slice, probe_field, offsets, assignment, intensities):
    depth_count = lax.axis_size("depth")
    depth_index = lax.axis_index("depth")
    rows_dev = object_slice.shape[2]
    cycles = object_slice.shape[1]
    patch_side = probe_field.shape[2]
    pos_count = assignment.shape[0]
    total_pos = pos_count * lax.axis_size("scan")
    band_rows = lax.all_gather(object_slice, "scan", axis=3, tiled=True)
    full_width = band_rows.shape[3]
    flat_band = band_rows.reshape(2, cycles * rows_dev, full_width)
    position = offsets[assignment]
    top_row = position[:, 0]
    left_col = position[:, 1]
    table_re, table_im = dft_table(patch_side)
    row_ids = jnp.arange(rows_dev, dtype=jnp.int32)
    col_ids = jnp.arange(patch_side, dtype=jnp.int32)
    col_cos, col_sin = chirp_phase(col_ids, patch_side)
    zero_start = jnp.int32(0)

    def cut_tile(cycle_row, column):
        return lax.dynamic_slice(
            flat_band, (zero_start, cycle_row * rows_dev, column), (2, rows_dev, patch_side)
        )

    block_first = top_row // rows_dev
    offset_in = top_row % rows_dev
    first_block = block_first + (depth_index - block_first) % depth_count
    first_cycle = first_block // depth_count
    second_cycle = jnp.minimum(first_cycle + 1, cycles - 1)
    pair_tiles = jnp.stack(
        [jax.vmap(cut_tile)(first_cycle, left_col), jax.vmap(cut_tile)(second_cycle, left_col)], 1
    )
    levels = depth_count.bit_length() - 1
    amount = (depth_count - block_first % depth_count) % depth_count
    for level in range(levels):
        moved = from_behind(pair_tiles, "depth", 1 << level)
        taken = amount >> level & 1 == 1
        pair_tiles = jnp.where(taken[:, None, None, None, None], moved, pair_tiles)
    first_tile = pair_tiles[:, 0]
    outgoing = jnp.where(depth_index == 0, pair_tiles[:, 1], first_tile)
    following = from_behind(outgoing, "depth", depth_count - 1)
    stacked = jnp.concatenate([first_tile, following], 2)

    def take_rows(tile_pair, corner_row):
        return lax.dynamic_slice_in_dim(tile_pair, corner_row, rows_dev, 1)

    patch = jax.vmap(take_rows)(stacked, offset_in)
    patch_rows = jnp.broadcast_to(depth_index * rows_dev + row_ids[None, :], (pos_count, rows_dev))
    probe_rows = lax.dynamic_slice_in_dim(probe_field, depth_index * rows_dev, rows_dev, 1)[None]
    row_cos, row_sin = chirp_phase(patch_rows, patch_side)
    chirp_re = (
        row_cos[:, :, None] * col_cos[None, None, :] - row_sin[:, :, None] * col_sin[None, None, :]
    )
    chirp_im = (
        row_sin[:, :, None] * col_cos[None, None, :] + row_cos[:, :, None] * col_sin[None, None, :]
    )
    obj_re = patch[:, 0].astype(jnp.float32)
    obj_im = patch[:, 1].astype(jnp.float32)
    probe_re = probe_rows[:, 0].astype(jnp.float32)
    probe_im = probe_rows[:, 1].astype(jnp.float32)
    wave_re = probe_re * obj_re - probe_im * obj_im
    wave_im = probe_re * obj_im + probe_im * obj_re
    psi_re = wave_re * chirp_re - wave_im * chirp_im
    psi_im = wave_re * chirp_im + wave_im * chirp_re
    half_re, half_im = complex_mix("vk,pjk->pvj", table_re, table_im, psi_re, psi_im)
    half_re, half_im = (
        lax.all_to_all(half_re, "depth", split_axis=1, concat_axis=2, tiled=True),
        lax.all_to_all(half_im, "depth", split_axis=1, concat_axis=2, tiled=True),
    )
    far_re, far_im = complex_mix("pvj,ju->pvu", half_re, half_im, table_re, table_im)
    excess = far_re * far_re + far_im * far_im - intensities
    resid_re = excess * far_re
    resid_im = excess * far_im
    mid_re, mid_im = complex_mix("pvu,uj->pvj", resid_re, resid_im, table_re, -table_im)
    mid_re, mid_im = (
        lax.all_to_all(mid_re, "depth", split_axis=2, concat_axis=1, tiled=True),
        lax.all_to_all(mid_im, "depth", split_axis=2, concat_axis=1, tiled=True),
    )
    back_re, back_im = complex_mix("vk,pvj->pjk", table_re, -table_im, mid_re, mid_im)
    grad_re = back_re * chirp_re + back_im * chirp_im
    grad_im = back_im * chirp_re - back_re * chirp_im
    contrib = jnp.stack(
        [probe_re * grad_re + probe_im * grad_im, probe_re * grad_im - probe_im * grad_re], 1
    )
    term_re = obj_re * grad_re + obj_im * grad_im
    term_im = obj_re * grad_im - obj_im * grad_re
    grad_band = jnp.zeros((2, cycles * rows_dev, full_width), jnp.float32)

    def add_tile(band_now, tile_value, cycle_row, column):
        corner = (zero_start, cycle_row * rows_dev, column)
        current = lax.dynamic_slice(band_now, corner, (2, rows_dev, patch_side))
        return lax.dynamic_update_slice(band_now, current + tile_value, corner)

    empty_window = jnp.zeros((pos_count, 2, 2 * rows_dev, patch_side), jnp.float32)

    def place_rows(window_zero, tile_rows, corner_row):
        return lax.dynamic_update_slice_in_dim(window_zero, tile_rows, corner_row, 1)

    placed = jax.vmap(place_rows)(empty_window, contrib, offset_in)
    head_part = placed[:, :, :rows_dev]
    tail_part = placed[:, :, rows_dev:]
    returned = from_behind(tail_part, "depth", 1)
    is_first = depth_index == 0
    head_part = jnp.where(is_first, head_part, head_part + returned)
    second_part = jnp.where(is_first, returned, jnp.zeros_like(returned))
    grad_pair = jnp.stack([head_part, second_part], 1)
    amount_back = block_first % depth_count
    for level in range(levels):
        moved_back = from_behind(grad_pair, "depth", 1 << level)
        taken_back = amount_back >> level & 1 == 1
        grad_pair = jnp.where(taken_back[:, None, None, None, None], moved_back, grad_pair)
    for slot_index in range(pos_count):
        grad_band = add_tile(
            grad_band, grad_pair[slot_index, 0], first_cycle[slot_index], left_col[slot_index]
        )
        grad_band = add_tile(
            grad_band, grad_pair[slot_index, 1], second_cycle[slot_index], left_col[slot_index]
        )
    probe_sum = jnp.stack([jnp.sum(term_re, 0), jnp.sum(term_im, 0)])
    probe_grad = lax.psum(probe_sum, "scan")
    object_grad = lax.psum_scatter(
        grad_band.reshape(2, cycles, rows_dev, full_width), "scan", scatter_dimension=3, tiled=True
    )
    return (object_grad, probe_grad * total_pos ** (-0.5))


def solution(mesh):
    return jax.shard_map(
        on_device,
        mesh=mesh,
        in_specs=(P(None, None, "depth", "scan"), P(), P(), P("scan"), P("scan", "depth", None)),
        out_specs=(P(None, None, "depth", "scan"), P(None, "depth", None)),
        check_vma=False,
    )
```

profile of v0, /device:TPU:8, one launch (start us, length us, event | category | flops | bytes accessed | tf_op | source)
XLA Modules:
  0.0 748.6 jit_solution(7698439106445803496)
XLA Ops:
  11.9 73.0 %all-gather.2.cloned.1.call-done = bf16[2,4,32,2048]{2,1,0,3:T(4,128)(2,1)} async-done(((bf16[2,4,32,64]{2,1,0,3:T(4,128)(2,1)}), bf16[2,4,32,2048]{2,1,0,3:T(4,128)(2,1)}) %all-gather.2.cloned.1.call-update) | async-done | bytes 1048592 | tf_op jit(solution)/shard_map/all_gather | solution.py:56
  85.0 5.5 copy.64
  102.9 6.9 collective-permute-done
  114.8 9.8 %collective-permute-done.1 = bf16[2,2,2,32,512]{4,2,0,3,1:T(2,128)(2,1)S(1)} collective-permute-done((bf16[2,2,2,32,512]{4,2,0,3,1:T(2,128)(2,1)S(1)}, bf16[2,2,2,32,512]{4,2,0,3,1:T(2,128)(2,1)S(1)}, u32[]{:S(2)}, u32[]{:S(2)}) %collective-permute-start.1) | collective-permute-done | bytes 262176 | tf_op jit(solution)/shard_map/ppermute | solution.py:13
  130.1 15.7 %collective-permute-done.2 = bf16[2,2,2,32,512]{4,2,0,3,1:T(2,128)(2,1)S(1)} collective-permute-done((bf16[2,2,2,32,512]{4,2,0,3,1:T(2,128)(2,1)S(1)}, bf16[2,2,2,32,512]{4,2,0,3,1:T(2,128)(2,1)S(1)}, u32[]{:S(2)}, u32[]{:S(2)}) %collective-permute-start.2) | collective-permute-done | bytes 262176 | tf_op jit(solution)/shard_map/ppermute | solution.py:13
  149.0 8.0 %collective-permute-done.3 = bf16[2,2,2,32,512]{4,2,0,3,1:T(2,128)(2,1)S(1)} collective-permute-done((bf16[2,2,2,32,512]{4,2,0,3,1:T(2,128)(2,1)S(1)}, bf16[2,2,2,32,512]{4,2,0,3,1:T(2,128)(2,1)S(1)}, u32[]{:S(2)}, u32[]{:S(2)}) %collective-permute-start.3) | collective-permute-done | bytes 262176 | tf_op jit(solution)/shard_map/ppermute | solution.py:13
  157.6 8.7 %collective-permute-start.4 = (bf16[2,2,32,512]{3,1,0,2:T(2,128)(2,1)S(1)}, bf16[2,2,32,512]{3,1,0,2:T(2,128)(2,1)S(1)}, u32[]{:S(2)}, u32[]{:S(2)}) collective-permute-start(bf16[2,2,32,512]{3,1,0,2:T(2,128)(2,1)S(1)} %broadcast_select_fusion.8), channel_id=1, source_target_pairs={{32,0},{64,32},{96,64},{128,96},{160,128},{192,160},{224,192},{256... | collective-permute-start | bytes 393224 | tf_op jit(solution)/shard_map/ppermute | solution.py:13
  186.7 7.4 all-to-all-start
  203.5 7.1 all-to-all-start.1
  250.2 9.6 %all-to-all-start.2 = ((f32[16,1,2048]{2,1,0:T(1,128)}), f32[16,1,2048]{2,1,0:T(1,128)S(1)}, u32[]{:S(2)}, u32[]{:S(2)}) async-start(f32[16,1,2048]{2,1,0:T(1,128)} %reshape.375), calls=%async_computation.2 | async-start | bytes 262144 | tf_op jit(solution)/shard_map/all_to_all | solution.py:124
  269.3 6.3 all-to-all-start.3
  301.8 14.5 %while.5 = (s32[]{:T(128)}, f32[2,2,64,512]{3,1,0,2:T(2,128)S(1)}, s32[2,4]{1,0:T(2,128)S(1)}, f32[2,2,32,512]{3,2,0,1:T(8,128)S(1)}, s32[]{:T(128)}, /*index=5*/s32[4]{0:T(128)S(1)}) while((s32[]{:T(128)}, f32[2,2,64,512]{3,1,0,2:T(2,128)S(1)}, s32[2,4]{1,0:T(2,128)S(1)}, f32[2,2,32,512]{3,2,0,1:T(8,128)S(1)}, s32[]{:T(128)}, ...), condition=%wide.while_cond.2, body=%wide.while_body.2.sunk | while | flops 32797 | bytes 917703 | solution.py:145
  318.9 5.6 collective-permute-done.5
  329.3 9.1 %collective-permute-done.6 = f32[2,2,2,32,512]{4,2,0,3,1:T(2,128)S(1)} collective-permute-done((f32[2,2,2,32,512]{4,2,0,3,1:T(2,128)S(1)}, f32[2,2,2,32,512]{4,2,0,3,1:T(2,128)S(1)}, u32[]{:S(2)}, u32[]{:S(2)}) %collective-permute-start.6) | collective-permute-done | bytes 524320 | tf_op jit(solution)/shard_map/ppermute | solution.py:13
  342.8 18.4 %collective-permute-done.7 = f32[2,2,2,32,512]{4,2,0,3,1:T(2,128)S(1)} collective-permute-done((f32[2,2,2,32,512]{4,2,0,3,1:T(2,128)S(1)}, f32[2,2,2,32,512]{4,2,0,3,1:T(2,128)S(1)}, u32[]{:S(2)}, u32[]{:S(2)}) %collective-permute-start.7) | collective-permute-done | bytes 524320 | tf_op jit(solution)/shard_map/ppermute | solution.py:13
  366.3 20.3 %collective-permute-done.8 = f32[2,2,2,32,512]{4,2,0,3,1:T(2,128)S(1)} collective-permute-done((f32[2,2,2,32,512]{4,2,0,3,1:T(2,128)S(1)}, f32[2,2,2,32,512]{4,2,0,3,1:T(2,128)S(1)}, u32[]{:S(2)}, u32[]{:S(2)}) %collective-permute-start.8) | collective-permute-done | bytes 524320 | tf_op jit(solution)/shard_map/ppermute | solution.py:13
  401.8 6.2 dynamic_update_slice.12
  409.1 6.2 dynamic_update_slice.13
  416.4 6.1 dynamic_update_slice.14
  423.7 6.1 dynamic_update_slice.15
  429.8 6.1 copy.84
  436.0 8.6 %reshape.365 = f32[2048,256]{1,0:T(8,128)} reshape(f32[2048,2,4,32]{3,2,1,0:T(4,128)} %bitcast.195) | data formatting | bytes 4194304
  444.6 169.5 %all-reduce.2.cloned.1.call-done = f32[2,32,512]{2,1,0:T(8,128)} async-done(((f32[2,32,512]{2,1,0:T(8,128)}), f32[2,32,512]{2,1,0:T(8,128)}) %all-reduce.2.cloned.1.call-update) | async-done | bytes 131088 | tf_op jit(solution)/shard_map/psum | solution.py:168
  615.6 124.2 %reduce-scatter.4.cloned.1.call-done = f32[64,256]{1,0:T(8,128)} async-done(((f32[2048,256]{1,0:T(8,128)}), f32[64,256]{1,0:T(8,128)}) %reduce-scatter.4.cloned.1.call-update) | async-done | bytes 65552
  (155 shorter events, 191.0 us)
Async XLA Ops:
  7.2 107.7 %copy-start = (bf16[2,512,512]{2,1,0:T(8,128)(2,1)S(1)}, bf16[2,512,512]{2,1,0:T(8,128)(2,1)}, u32[]{:S(2)}) copy-start(bf16[2,512,512]{2,1,0:T(8,128)(2,1)} %param.6) | copy-start | bytes 3145732
  7.2 77.8 %all-gather.2.cloned.1.call-start = ((), (), s32[]{:S(2)}) async-start(), calls=%async_computation.5 | async-start | bytes 4325376 | tf_op jit(solution)/shard_map/all_gather | solution.py:56
  99.4 10.3 %collective-permute-start = (bf16[2,2,2,32,512]{4,2,0,3,1:T(2,128)(2,1)S(1)}, bf16[2,2,2,32,512]{4,2,0,3,1:T(2,128)(2,1)S(1)}, u32[]{:S(2)}, u32[]{:S(2)}) collective-permute-start(bf16[2,2,2,32,512]{4,2,0,3,1:T(2,128)(2,1)S(1)} %pad_maximum_fusion.1), channel_id=1, source_target_pairs={{480,0},{0,32},{32,64},{64,96},{96,128},{128,160},{160,192},{192,2... | collective-permute-start | bytes 786440 | tf_op jit(solution)/shard_map/ppermute | solution.py:13
  110.3 14.4 %collective-permute-start.1 = (bf16[2,2,2,32,512]{4,2,0,3,1:T(2,128)(2,1)S(1)}, bf16[2,2,2,32,512]{4,2,0,3,1:T(2,128)(2,1)S(1)}, u32[]{:S(2)}, u32[]{:S(2)}) collective-permute-start(bf16[2,2,2,32,512]{4,2,0,3,1:T(2,128)(2,1)S(1)} %broadcast_select_fusion.4), channel_id=1, source_target_pairs={{448,0},{480,32},{0,64},{32,96},{64,128},{96,160},{128,192},{160,2... | collective-permute-start | bytes 786440 | tf_op jit(solution)/shard_map/ppermute | solution.py:13
  125.3 20.5 %collective-permute-start.2 = (bf16[2,2,2,32,512]{4,2,0,3,1:T(2,128)(2,1)S(1)}, bf16[2,2,2,32,512]{4,2,0,3,1:T(2,128)(2,1)S(1)}, u32[]{:S(2)}, u32[]{:S(2)}) collective-permute-start(bf16[2,2,2,32,512]{4,2,0,3,1:T(2,128)(2,1)S(1)} %broadcast_select_fusion.5), channel_id=1, source_target_pairs={{384,0},{416,32},{448,64},{480,96},{0,128},{32,160},{64,192},{96,2... | collective-permute-start | bytes 786440 | tf_op jit(solution)/shard_map/ppermute | solution.py:13
  146.2 10.9 %collective-permute-start.3 = (bf16[2,2,2,32,512]{4,2,0,3,1:T(2,128)(2,1)S(1)}, bf16[2,2,2,32,512]{4,2,0,3,1:T(2,128)(2,1)S(1)}, u32[]{:S(2)}, u32[]{:S(2)}) collective-permute-start(bf16[2,2,2,32,512]{4,2,0,3,1:T(2,128)(2,1)S(1)} %broadcast_select_fusion.6), channel_id=1, source_target_pairs={{256,0},{288,32},{320,64},{352,96},{384,128},{416,160},{448,192},{... | collective-permute-start | bytes 786440 | tf_op jit(solution)/shard_map/ppermute | solution.py:13
  157.6 11.0 %collective-permute-start.4 = (bf16[2,2,32,512]{3,1,0,2:T(2,128)(2,1)S(1)}, bf16[2,2,32,512]{3,1,0,2:T(2,128)(2,1)S(1)}, u32[]{:S(2)}, u32[]{:S(2)}) collective-permute-start(bf16[2,2,32,512]{3,1,0,2:T(2,128)(2,1)S(1)} %broadcast_select_fusion.8), channel_id=1, source_target_pairs={{32,0},{64,32},{96,64},{128,96},{160,128},{192,160},{224,192},{256... | collective-permute-start | bytes 393224 | tf_op jit(solution)/shard_map/ppermute | solution.py:13
  186.7 16.9 %all-to-all-start = ((f32[16,1,2048]{2,1,0:T(1,128)}), f32[16,1,2048]{2,1,0:T(1,128)S(1)}, u32[]{:S(2)}, u32[]{:S(2)}) async-start(f32[16,1,2048]{2,1,0:T(1,128)} %reshape.369), calls=%async_computation | async-start | bytes 262144 | tf_op jit(solution)/shard_map/all_to_all | solution.py:115
  203.5 19.1 %all-to-all-start.1 = ((f32[16,1,2048]{2,1,0:T(1,128)}), f32[16,1,2048]{2,1,0:T(1,128)S(1)}, u32[]{:S(2)}, u32[]{:S(2)}) async-start(f32[16,1,2048]{2,1,0:T(1,128)} %reshape.371), calls=%async_computation.1 | async-start | bytes 262144 | tf_op jit(solution)/shard_map/all_to_all | solution.py:116
  229.3 5.0 copy-start.3
  250.2 19.1 %all-to-all-start.2 = ((f32[16,1,2048]{2,1,0:T(1,128)}), f32[16,1,2048]{2,1,0:T(1,128)S(1)}, u32[]{:S(2)}, u32[]{:S(2)}) async-start(f32[16,1,2048]{2,1,0:T(1,128)} %reshape.375), calls=%async_computation.2 | async-start | bytes 262144 | tf_op jit(solution)/shard_map/all_to_all | solution.py:124
  269.3 15.8 %all-to-all-start.3 = ((f32[16,1,2048]{2,1,0:T(1,128)}), f32[16,1,2048]{2,1,0:T(1,128)S(1)}, u32[]{:S(2)}, u32[]{:S(2)}) async-start(f32[16,1,2048]{2,1,0:T(1,128)} %reshape.373), calls=%async_computation.3 | async-start | bytes 262144 | tf_op jit(solution)/shard_map/all_to_all | solution.py:125
  275.6 338.4 %all-reduce.2.cloned.1.call-start = ((), (), s32[]{:S(2)}) async-start(), calls=%async_computation.6 | async-start | bytes 262144 | tf_op jit(solution)/shard_map/psum | solution.py:168
  296.6 5.1 copy-start.2
  316.3 8.3 %collective-permute-start.5 = (f32[2,2,32,512]{3,1,0,2:T(2,128)S(1)}, f32[2,2,32,512]{3,1,0,2:T(2,128)S(1)}, u32[]{:S(2)}, u32[]{:S(2)}) collective-permute-start(f32[2,2,32,512]{3,1,0,2:T(2,128)S(1)} %slice.75), channel_id=1, source_target_pairs={{480,0},{0,32},{32,64},{64,96},{96,128},{128,160},{160,192},{192,2... | collective-permute-start | bytes 786440 | tf_op jit(solution)/shard_map/ppermute | solution.py:13
  325.0 13.3 %collective-permute-start.6 = (f32[2,2,2,32,512]{4,2,0,3,1:T(2,128)S(1)}, f32[2,2,2,32,512]{4,2,0,3,1:T(2,128)S(1)}, u32[]{:S(2)}, u32[]{:S(2)}) collective-permute-start(f32[2,2,2,32,512]{4,2,0,3,1:T(2,128)S(1)} %pad_maximum_fusion), channel_id=1, source_target_pairs={{480,0},{0,32},{32,64},{64,96},{96,128},{128,160},{160,192},{192,2... | collective-permute-start | bytes 1572872 | tf_op jit(solution)/shard_map/ppermute | solution.py:13
  338.8 22.4 %collective-permute-start.7 = (f32[2,2,2,32,512]{4,2,0,3,1:T(2,128)S(1)}, f32[2,2,2,32,512]{4,2,0,3,1:T(2,128)S(1)}, u32[]{:S(2)}, u32[]{:S(2)}) collective-permute-start(f32[2,2,2,32,512]{4,2,0,3,1:T(2,128)S(1)} %broadcast_select_fusion), channel_id=1, source_target_pairs={{448,0},{480,32},{0,64},{32,96},{64,128},{96,160},{128,192},{160,2... | collective-permute-start | bytes 1572872 | tf_op jit(solution)/shard_map/ppermute | solution.py:13
  361.6 25.0 %collective-permute-start.8 = (f32[2,2,2,32,512]{4,2,0,3,1:T(2,128)S(1)}, f32[2,2,2,32,512]{4,2,0,3,1:T(2,128)S(1)}, u32[]{:S(2)}, u32[]{:S(2)}) collective-permute-start(f32[2,2,2,32,512]{4,2,0,3,1:T(2,128)S(1)} %broadcast_select_fusion.1), channel_id=1, source_target_pairs={{384,0},{416,32},{448,64},{480,96},{0,128},{32,160},{64,192},{96,2... | collective-permute-start | bytes 1572872 | tf_op jit(solution)/shard_map/ppermute | solution.py:13
  387.0 12.6 %collective-permute-start.9 = (f32[2,2,2,32,512]{4,2,0,3,1:T(2,128)S(1)}, f32[2,2,2,32,512]{4,2,0,3,1:T(2,128)S(1)}, u32[]{:S(2)}, u32[]{:S(2)}) collective-permute-start(f32[2,2,2,32,512]{4,2,0,3,1:T(2,128)S(1)} %broadcast_select_fusion.2), channel_id=1, source_target_pairs={{256,0},{288,32},{320,64},{352,96},{384,128},{416,160},{448,192},{... | collective-permute-start | bytes 1572872 | tf_op jit(solution)/shard_map/ppermute | solution.py:13
  397.2 342.6 %reduce-scatter.4.cloned.1.call-start = ((), (), s32[]{:S(2)}) async-start(), calls=%async_computation.7 | async-start | bytes 2162688
  399.9 0.8 copy-start.1
Sparse Core Ops, SparseCore 0:
  10.7 74.1 all-gather.1
  397.4 216.6 all-reduce.1
  616.8 122.9 reduce-scatter.3
where the time goes:
time: 754 us; the launch traced here: 749 us
  waiting for transfers between devices  474 us (63%)
  local copies, waits for them, and re-layouts  79.3 us (11%)
  matrix products  78 us (10%)
  starting transfers between devices  72.2 us (10%)
  other arithmetic  23.6 us (3%)
  between operations  21.3 us (3%)
    psum x1, waiting for transfers between devices, on_device(): probe_grad = lax.psum(probe_sum, 'scan')  169 us
    unnamed x4, waiting for transfers between devices  124 us
    ppermute x10, waiting for transfers between devices, from_behind(): return lax.ppermute(block, axis, route)  98.4 us
    dot_general x16, matrix products, contract(): jnp.einsum(form, left_side, right_side, precision=lax.Precision.HIGHEST,...  78 us
    all_gather x1, waiting for transfers between devices, on_device(): band_rows = lax.all_gather(object_slice, 'scan', axis=3, tiled=True)  73 us
    ppermute x10, starting transfers between devices, from_behind(): return lax.ppermute(block, axis, route)  41.7 us
    unnamed x26, local copies, waits for them, and re-layouts  26.5 us
    dynamic_update_slice x4, local copies, waits for them, and re-layouts, add_tile(): return lax.dynamic_update_slice(band_now, current + tile_value, corner)  24.7 us
  transfers between devices with their start and end apart: 17, of which 16 were waited for; matrix products, arithmetic and copies ran while one was open for 11% of the time, Pallas kernels for 0%

commit v1 on v0

--- a/solution.py
+++ b/solution.py
@@ -53,7 +53,9 @@
     patch_side = probe_field.shape[2]
     pos_count = assignment.shape[0]
     total_pos = pos_count * lax.axis_size("scan")
-    band_rows = lax.all_gather(object_slice, "scan", axis=3, tiled=True)
+    band_rows = jnp.concatenate(
+        lax.all_to_all(jnp.stack([object_slice] * lax.axis_size("scan")), "scan", 0, 0), axis=3
+    )
     full_width = band_rows.shape[3]
     flat_band = band_rows.reshape(2, cycles * rows_dev, full_width)
     position = offsets[assignment]

time: 754 us -> 726 us (0.963)
  waiting for transfers between devices: 474 us -> 424 us
  starting transfers between devices: 72.2 us -> 86.1 us
    all_gather x1 -> x0, waiting for transfers between devices: 73 us -> none  [on_device(): band_rows = lax.all_gather(object_slice, 'scan', axis=3, tiled=True)]
    all_to_all x0 -> x1, waiting for transfers between devices: none -> 27.5 us  [on_device(): lax.all_to_all(jnp.stack([object_slice] * lax.axis_size('scan')), 'scan',...]
    all_to_all x0 -> x1, starting transfers between devices: none -> 11.8 us  [on_device(): lax.all_to_all(jnp.stack([object_slice] * lax.axis_size('scan')), 'scan',...]
    unnamed x26 -> x33, local copies, waits for them, and re-layouts: 26.5 us -> 30.2 us
    unnamed x4 -> x3, waiting for transfers between devices: 124 us -> 124 us
where the time goes in v1:
time: 726 us; the launch traced here: 718 us
  waiting for transfers between devices  424 us (58%)
  starting transfers between devices  86.1 us (12%)
  local copies, waits for them, and re-layouts  85.2 us (12%)
  matrix products  78 us (11%)
  other arithmetic  22.3 us (3%)
  between operations  21.6 us (3%)
    psum x1, waiting for transfers between devices, on_device(): probe_grad = lax.psum(probe_sum, 'scan')  169 us
    unnamed x3, waiting for transfers between devices  124 us
    ppermute x10, waiting for transfers between devices, from_behind(): return lax.ppermute(block, axis, route)  94.9 us
    dot_general x16, matrix products, contract(): jnp.einsum(form, left_side, right_side, precision=lax.Precision.HIGHEST,...  78 us
    ppermute x10, starting transfers between devices, from_behind(): return lax.ppermute(block, axis, route)  43.9 us
    unnamed x33, local copies, waits for them, and re-layouts  30.2 us
    all_to_all x1, waiting for transfers between devices, on_device(): lax.all_to_all(jnp.stack([object_slice] * lax.axis_size('scan')), 'scan',...  27.5 us
    dynamic_update_slice x4, local copies, waits for them, and re-layouts, add_tile(): return lax.dynamic_update_slice(band_now, current + tile_value, corner)  24.7 us
  transfers between devices with their start and end apart: 17, of which 16 were waited for; matrix products, arithmetic and copies ran while one was open for 11% of the time, Pallas kernels for 0%

profile of v1, /device:TPU:8, one launch (start us, length us, event | category | flops | bytes accessed | tf_op | source)
XLA Modules:
  0.0 717.8 jit_solution(3329571264122866601)
XLA Ops:
  10.9 11.8 %all-to-all-start = ((bf16[32,2,8192]{2,1,0:T(2,128)(2,1)}), bf16[32,2,8192]{2,1,0:T(2,128)(2,1)}, u32[]{:S(2)}, u32[]{:S(2)}) async-start(bf16[32,2,8192]{2,1,0:T(2,128)(2,1)} %reshape.371), calls=%async_computation | async-start | bytes 2097152 | tf_op jit(solution)/shard_map/all_to_all | solution.py:57
  23.7 27.5 %all-to-all-done = bf16[32,2,8192]{2,1,0:T(2,128)(2,1)} async-done(((bf16[32,2,8192]{2,1,0:T(2,128)(2,1)}), bf16[32,2,8192]{2,1,0:T(2,128)(2,1)}, u32[]{:S(2)}, u32[]{:S(2)}) %all-to-all-start) | async-done | bytes 1048608 | tf_op jit(solution)/shard_map/all_to_all | solution.py:57
  73.7 6.3 collective-permute-done
  85.4 9.0 %collective-permute-done.1 = bf16[2,2,2,32,512]{4,2,0,3,1:T(2,128)(2,1)S(1)} collective-permute-done((bf16[2,2,2,32,512]{4,2,0,3,1:T(2,128)(2,1)S(1)}, bf16[2,2,2,32,512]{4,2,0,3,1:T(2,128)(2,1)S(1)}, u32[]{:S(2)}, u32[]{:S(2)}) %collective-permute-start.1) | collective-permute-done | bytes 262176 | tf_op jit(solution)/shard_map/ppermute | solution.py:13
  100.1 14.7 %collective-permute-done.2 = bf16[2,2,2,32,512]{4,2,0,3,1:T(2,128)(2,1)S(1)} collective-permute-done((bf16[2,2,2,32,512]{4,2,0,3,1:T(2,128)(2,1)S(1)}, bf16[2,2,2,32,512]{4,2,0,3,1:T(2,128)(2,1)S(1)}, u32[]{:S(2)}, u32[]{:S(2)}) %collective-permute-start.2) | collective-permute-done | bytes 262176 | tf_op jit(solution)/shard_map/ppermute | solution.py:13
  118.8 6.4 collective-permute-done.3
  125.7 11.2 %collective-permute-start.4 = (bf16[2,2,32,512]{3,1,0,2:T(2,128)(2,1)S(1)}, bf16[2,2,32,512]{3,1,0,2:T(2,128)(2,1)S(1)}, u32[]{:S(2)}, u32[]{:S(2)}) collective-permute-start(bf16[2,2,32,512]{3,1,0,2:T(2,128)(2,1)S(1)} %broadcast_select_fusion.8), channel_id=1, source_target_pairs={{32,0},{64,32},{96,64},{128,96},{160,128},{192,160},{224,192},{256... | collective-permute-start | bytes 393224 | tf_op jit(solution)/shard_map/ppermute | solution.py:13
  157.3 7.4 %all-to-all-start.1 = ((f32[16,1,2048]{2,1,0:T(1,128)}), f32[16,1,2048]{2,1,0:T(1,128)S(1)}, u32[]{:S(2)}, u32[]{:S(2)}) async-start(f32[16,1,2048]{2,1,0:T(1,128)} %reshape.373), calls=%async_computation.1 | async-start | bytes 262144 | tf_op jit(solution)/shard_map/all_to_all | solution.py:117
  174.2 7.1 all-to-all-start.2
  220.9 9.6 %all-to-all-start.3 = ((f32[16,1,2048]{2,1,0:T(1,128)}), f32[16,1,2048]{2,1,0:T(1,128)S(1)}, u32[]{:S(2)}, u32[]{:S(2)}) async-start(f32[16,1,2048]{2,1,0:T(1,128)} %reshape.379), calls=%async_computation.3 | async-start | bytes 262144 | tf_op jit(solution)/shard_map/all_to_all | solution.py:126
  240.1 6.3 all-to-all-start.4
  272.5 14.5 %while.5 = (s32[]{:T(128)}, f32[2,2,64,512]{3,1,0,2:T(2,128)S(1)}, s32[2,4]{1,0:T(2,128)S(1)}, f32[2,2,32,512]{3,2,0,1:T(8,128)S(1)}, s32[]{:T(128)}, /*index=5*/s32[4]{0:T(128)S(1)}) while((s32[]{:T(128)}, f32[2,2,64,512]{3,1,0,2:T(2,128)S(1)}, s32[2,4]{1,0:T(2,128)S(1)}, f32[2,2,32,512]{3,2,0,1:T(8,128)S(1)}, s32[]{:T(128)}, ...), condition=%wide.while_cond.2, body=%wide.while_body.2.sunk | while | flops 32797 | bytes 917703 | solution.py:147
  289.7 5.6 collective-permute-done.5
  299.7 9.4 %collective-permute-done.6 = f32[2,2,2,32,512]{4,2,0,3,1:T(2,128)S(1)} collective-permute-done((f32[2,2,2,32,512]{4,2,0,3,1:T(2,128)S(1)}, f32[2,2,2,32,512]{4,2,0,3,1:T(2,128)S(1)}, u32[]{:S(2)}, u32[]{:S(2)}) %collective-permute-start.6) | collective-permute-done | bytes 524320 | tf_op jit(solution)/shard_map/ppermute | solution.py:13
  312.4 21.0 %collective-permute-done.7 = f32[2,2,2,32,512]{4,2,0,3,1:T(2,128)S(1)} collective-permute-done((f32[2,2,2,32,512]{4,2,0,3,1:T(2,128)S(1)}, f32[2,2,2,32,512]{4,2,0,3,1:T(2,128)S(1)}, u32[]{:S(2)}, u32[]{:S(2)}) %collective-permute-start.7) | collective-permute-done | bytes 524320 | tf_op jit(solution)/shard_map/ppermute | solution.py:13
  337.1 19.0 %collective-permute-done.8 = f32[2,2,2,32,512]{4,2,0,3,1:T(2,128)S(1)} collective-permute-done((f32[2,2,2,32,512]{4,2,0,3,1:T(2,128)S(1)}, f32[2,2,2,32,512]{4,2,0,3,1:T(2,128)S(1)}, u32[]{:S(2)}, u32[]{:S(2)}) %collective-permute-start.8) | collective-permute-done | bytes 524320 | tf_op jit(solution)/shard_map/ppermute | solution.py:13
  371.2 6.2 dynamic_update_slice.12
  378.5 6.2 dynamic_update_slice.13
  385.8 6.1 dynamic_update_slice.14
  393.1 6.1 dynamic_update_slice.15
  399.2 6.1 copy.80
  405.4 8.6 %reshape.367 = f32[2048,256]{1,0:T(8,128)} reshape(f32[2048,2,4,32]{3,2,1,0:T(4,128)} %bitcast.197) | data formatting | bytes 4194304
  414.0 169.0 %all-reduce.2.cloned.1.call-done = f32[2,32,512]{2,1,0:T(8,128)} async-done(((f32[2,32,512]{2,1,0:T(8,128)}), f32[2,32,512]{2,1,0:T(8,128)}) %all-reduce.2.cloned.1.call-update) | async-done | bytes 131088 | tf_op jit(solution)/shard_map/psum | solution.py:170
  584.5 124.2 %reduce-scatter.4.cloned.1.call-done = f32[64,256]{1,0:T(8,128)} async-done(((f32[2048,256]{1,0:T(8,128)}), f32[64,256]{1,0:T(8,128)}) %reduce-scatter.4.cloned.1.call-update) | async-done | bytes 65552
  (163 shorter events, 199.6 us)
Async XLA Ops:
  7.2 78.2 %copy-start = (bf16[2,512,512]{2,1,0:T(8,128)(2,1)S(1)}, bf16[2,512,512]{2,1,0:T(8,128)(2,1)}, u32[]{:S(2)}) copy-start(bf16[2,512,512]{2,1,0:T(8,128)(2,1)} %param.6) | copy-start | bytes 3145732
  8.6 14.1 %copy-start.3 = (s32[64,2]{0,1:T(2,128)S(1)}, s32[64,2]{0,1:T(2,128)}, u32[]{:S(2)}) copy-start(s32[64,2]{0,1:T(2,128)} %param.7) | copy-start | bytes 1540
  8.6 14.2 %copy-start.6 = (s32[2]{0:T(128)S(1)}, s32[2]{0:T(128)}, u32[]{:S(2)}) copy-start(s32[2]{0:T(128)} %param.8) | copy-start | bytes 28
  8.6 15.0 %copy-start.4 = (s32[3]{0:T(128)S(1)}, s32[3]{0:T(128)}, u32[]{:S(2)}) copy-start(s32[3]{0:T(128)} %constant.136.clone.1) | copy-start | bytes 40
  10.9 40.3 %all-to-all-start = ((bf16[32,2,8192]{2,1,0:T(2,128)(2,1)}), bf16[32,2,8192]{2,1,0:T(2,128)(2,1)}, u32[]{:S(2)}, u32[]{:S(2)}) async-start(bf16[32,2,8192]{2,1,0:T(2,128)(2,1)} %reshape.371), calls=%async_computation | async-start | bytes 2097152 | tf_op jit(solution)/shard_map/all_to_all | solution.py:57
  70.2 9.9 %collective-permute-start = (bf16[2,2,2,32,512]{4,2,0,3,1:T(2,128)(2,1)S(1)}, bf16[2,2,2,32,512]{4,2,0,3,1:T(2,128)(2,1)S(1)}, u32[]{:S(2)}, u32[]{:S(2)}) collective-permute-start(bf16[2,2,2,32,512]{4,2,0,3,1:T(2,128)(2,1)S(1)} %pad_maximum_fusion.1), channel_id=1, source_target_pairs={{480,0},{0,32},{32,64},{64,96},{96,128},{128,160},{160,192},{192,2... | collective-permute-start | bytes 786440 | tf_op jit(solution)/shard_map/ppermute | solution.py:13
  80.5 13.9 %collective-permute-start.1 = (bf16[2,2,2,32,512]{4,2,0,3,1:T(2,128)(2,1)S(1)}, bf16[2,2,2,32,512]{4,2,0,3,1:T(2,128)(2,1)S(1)}, u32[]{:S(2)}, u32[]{:S(2)}) collective-permute-start(bf16[2,2,2,32,512]{4,2,0,3,1:T(2,128)(2,1)S(1)} %broadcast_select_fusion.4), channel_id=1, source_target_pairs={{448,0},{480,32},{0,64},{32,96},{64,128},{96,160},{128,192},{160,2... | collective-permute-start | bytes 786440 | tf_op jit(solution)/shard_map/ppermute | solution.py:13
  95.0 19.8 %collective-permute-start.2 = (bf16[2,2,2,32,512]{4,2,0,3,1:T(2,128)(2,1)S(1)}, bf16[2,2,2,32,512]{4,2,0,3,1:T(2,128)(2,1)S(1)}, u32[]{:S(2)}, u32[]{:S(2)}) collective-permute-start(bf16[2,2,2,32,512]{4,2,0,3,1:T(2,128)(2,1)S(1)} %broadcast_select_fusion.5), channel_id=1, source_target_pairs={{384,0},{416,32},{448,64},{480,96},{0,128},{32,160},{64,192},{96,2... | collective-permute-start | bytes 786440 | tf_op jit(solution)/shard_map/ppermute | solution.py:13
  115.1 10.1 %collective-permute-start.3 = (bf16[2,2,2,32,512]{4,2,0,3,1:T(2,128)(2,1)S(1)}, bf16[2,2,2,32,512]{4,2,0,3,1:T(2,128)(2,1)S(1)}, u32[]{:S(2)}, u32[]{:S(2)}) collective-permute-start(bf16[2,2,2,32,512]{4,2,0,3,1:T(2,128)(2,1)S(1)} %broadcast_select_fusion.6), channel_id=1, source_target_pairs={{256,0},{288,32},{320,64},{352,96},{384,128},{416,160},{448,192},{... | collective-permute-start | bytes 786440 | tf_op jit(solution)/shard_map/ppermute | solution.py:13
  125.7 13.5 %collective-permute-start.4 = (bf16[2,2,32,512]{3,1,0,2:T(2,128)(2,1)S(1)}, bf16[2,2,32,512]{3,1,0,2:T(2,128)(2,1)S(1)}, u32[]{:S(2)}, u32[]{:S(2)}) collective-permute-start(bf16[2,2,32,512]{3,1,0,2:T(2,128)(2,1)S(1)} %broadcast_select_fusion.8), channel_id=1, source_target_pairs={{32,0},{64,32},{96,64},{128,96},{160,128},{192,160},{224,192},{256... | collective-permute-start | bytes 393224 | tf_op jit(solution)/shard_map/ppermute | solution.py:13
  157.3 16.9 %all-to-all-start.1 = ((f32[16,1,2048]{2,1,0:T(1,128)}), f32[16,1,2048]{2,1,0:T(1,128)S(1)}, u32[]{:S(2)}, u32[]{:S(2)}) async-start(f32[16,1,2048]{2,1,0:T(1,128)} %reshape.373), calls=%async_computation.1 | async-start | bytes 262144 | tf_op jit(solution)/shard_map/all_to_all | solution.py:117
  174.2 19.2 %all-to-all-start.2 = ((f32[16,1,2048]{2,1,0:T(1,128)}), f32[16,1,2048]{2,1,0:T(1,128)S(1)}, u32[]{:S(2)}, u32[]{:S(2)}) async-start(f32[16,1,2048]{2,1,0:T(1,128)} %reshape.375), calls=%async_computation.2 | async-start | bytes 262144 | tf_op jit(solution)/shard_map/all_to_all | solution.py:118
  200.1 5.0 copy-start.5
  220.9 19.1 %all-to-all-start.3 = ((f32[16,1,2048]{2,1,0:T(1,128)}), f32[16,1,2048]{2,1,0:T(1,128)S(1)}, u32[]{:S(2)}, u32[]{:S(2)}) async-start(f32[16,1,2048]{2,1,0:T(1,128)} %reshape.379), calls=%async_computation.3 | async-start | bytes 262144 | tf_op jit(solution)/shard_map/all_to_all | solution.py:126
  240.1 15.8 %all-to-all-start.4 = ((f32[16,1,2048]{2,1,0:T(1,128)}), f32[16,1,2048]{2,1,0:T(1,128)S(1)}, u32[]{:S(2)}, u32[]{:S(2)}) async-start(f32[16,1,2048]{2,1,0:T(1,128)} %reshape.377), calls=%async_computation.4 | async-start | bytes 262144 | tf_op jit(solution)/shard_map/all_to_all | solution.py:127
  246.4 336.6 %all-reduce.2.cloned.1.call-start = ((), (), s32[]{:S(2)}) async-start(), calls=%async_computation.6 | async-start | bytes 262144 | tf_op jit(solution)/shard_map/psum | solution.py:170
  267.4 5.1 copy-start.2
  287.0 8.3 %collective-permute-start.5 = (f32[2,2,32,512]{3,1,0,2:T(2,128)S(1)}, f32[2,2,32,512]{3,1,0,2:T(2,128)S(1)}, u32[]{:S(2)}, u32[]{:S(2)}) collective-permute-start(f32[2,2,32,512]{3,1,0,2:T(2,128)S(1)} %slice.75), channel_id=1, source_target_pairs={{480,0},{0,32},{32,64},{64,96},{96,128},{128,160},{160,192},{192,2... | collective-permute-start | bytes 786440 | tf_op jit(solution)/shard_map/ppermute | solution.py:13
  295.8 13.3 %collective-permute-start.6 = (f32[2,2,2,32,512]{4,2,0,3,1:T(2,128)S(1)}, f32[2,2,2,32,512]{4,2,0,3,1:T(2,128)S(1)}, u32[]{:S(2)}, u32[]{:S(2)}) collective-permute-start(f32[2,2,2,32,512]{4,2,0,3,1:T(2,128)S(1)} %pad_maximum_fusion), channel_id=1, source_target_pairs={{480,0},{0,32},{32,64},{64,96},{96,128},{128,160},{160,192},{192,2... | collective-permute-start | bytes 1572872 | tf_op jit(solution)/shard_map/ppermute | solution.py:13
  309.5 24.0 %collective-permute-start.7 = (f32[2,2,2,32,512]{4,2,0,3,1:T(2,128)S(1)}, f32[2,2,2,32,512]{4,2,0,3,1:T(2,128)S(1)}, u32[]{:S(2)}, u32[]{:S(2)}) collective-permute-start(f32[2,2,2,32,512]{4,2,0,3,1:T(2,128)S(1)} %broadcast_select_fusion), channel_id=1, source_target_pairs={{448,0},{480,32},{0,64},{32,96},{64,128},{96,160},{128,192},{160,2... | collective-permute-start | bytes 1572872 | tf_op jit(solution)/shard_map/ppermute | solution.py:13
  334.0 22.1 %collective-permute-start.8 = (f32[2,2,2,32,512]{4,2,0,3,1:T(2,128)S(1)}, f32[2,2,2,32,512]{4,2,0,3,1:T(2,128)S(1)}, u32[]{:S(2)}, u32[]{:S(2)}) collective-permute-start(f32[2,2,2,32,512]{4,2,0,3,1:T(2,128)S(1)} %broadcast_select_fusion.1), channel_id=1, source_target_pairs={{384,0},{416,32},{448,64},{480,96},{0,128},{32,160},{64,192},{96,2... | collective-permute-start | bytes 1572872 | tf_op jit(solution)/shard_map/ppermute | solution.py:13
  356.4 12.6 %collective-permute-start.9 = (f32[2,2,2,32,512]{4,2,0,3,1:T(2,128)S(1)}, f32[2,2,2,32,512]{4,2,0,3,1:T(2,128)S(1)}, u32[]{:S(2)}, u32[]{:S(2)}) collective-permute-start(f32[2,2,2,32,512]{4,2,0,3,1:T(2,128)S(1)} %broadcast_select_fusion.2), channel_id=1, source_target_pairs={{256,0},{288,32},{320,64},{352,96},{384,128},{416,160},{448,192},{... | collective-permute-start | bytes 1572872 | tf_op jit(solution)/shard_map/ppermute | solution.py:13
  367.8 340.9 %reduce-scatter.4.cloned.1.call-start = ((), (), s32[]{:S(2)}) async-start(), calls=%async_computation.7 | async-start | bytes 2162688
  369.3 0.8 copy-start.1
Sparse Core Ops, SparseCore 0:
  368.0 214.9 all-reduce.1
  585.8 122.8 reduce-scatter.3
